TPU v7x, 32 devices: a whole 2x2x4 slice. The times are simulated.
32 devices in a mesh: gx: 8 (over z, x), gy: 4 (over y, core).
Axes of the slice: x: 2, y: 2, z: 4, core: 2. Of those that a mesh axis runs over, the one named last changes fastest.
Arguments:
- fields: bfloat16 [4, 64, 128, 256], P(None, 'gx', 'gy'), may hold values from -6 to 6
- rows_live: int32 [8], replicated, may hold values from 4 to 8, as said below
- cols_live: int32 [4], replicated, may hold values from 16 to 32, as said below
- weight: bfloat16 [32, 108], replicated, may hold values from -0.625 to 0.625
- bias: float32 [32], replicated, may hold values from -3 to 3
- grad_out: bfloat16 [32, 32, 64, 128], P('gy', 'gx'), may hold values from -0.0625 to 0.0625
Outputs:
- stem: bfloat16 [32, 32, 64, 128], P('gy', 'gx')
- weight_grad: float32 [32, 108], P('gy')
- bias_grad: float32 [32], P('gy')
Inputs may be any that keep to these rules, and one draw needn't show every extreme that they name: `rows_live`: every entry is even, and some entry equals 8. `cols_live`: every entry is even, and some entry equals 32.
All inputs are finite; a program needn't handle non-finite values.
Results may differ from a plain program's by a relative error of at most 0.0054.
Values may be sent and summed in bfloat16 or wider, within the bound.
No kernel may reach another device: no remote copies, remote signals or barrier semaphores. Data moves between devices by JAX's collectives and lax.ppermute only.
A program may use at most 64 MiB of HBM per device.

v0:
```python
import jax
import jax.numpy as jnp
from jax import lax
from jax.sharding import PartitionSpec as P


def from_behind(block, axis, distance):
    devices = range(lax.axis_size(axis))
    route = [(i - distance, i) for i in devices if i - distance in devices]
    return lax.ppermute(block, axis, route)


def extend(data, border, count, dim):
    length = data.shape[dim]
    border_wide = jnp.expand_dims(border, dim)
    joined = jnp.concatenate([jnp.zeros_like(border_wide), data], axis=dim)
    shape = [1] * joined.ndim
    shape[dim] = length + 1
    places = jnp.arange(length + 1, dtype=jnp.int32).reshape(shape)
    edge_at = length - count
    kept = jnp.where(places > edge_at, joined, jnp.zeros_like(joined))
    return jnp.where(places == edge_at, border_wide, kept)


def taps(padded, axes, halves):
    pieces = []
    for off_x in range(3):
        for off_y in range(3):
            for off_z in range(3):
                piece = padded
                for axis_no, offset, half in zip(axes, (off_x, off_y, off_z), halves):
                    piece = lax.slice_in_dim(piece, offset, offset + 2 * half - 1, 2, axis_no)
                pieces.append(piece)
    return pieces


def local(fields, rows_live, cols_live, weight, bias, grad_out):
    in_chans, cap_x, cap_y, depth = fields.shape
    half_x = cap_x // 2
    half_y = cap_y // 2
    half_z = depth // 2
    out_chans = weight.shape[0]
    tiles_y = lax.axis_size("gy")
    row_count = rows_live[lax.axis_index("gx")]
    above = from_behind(fields[:, cap_x - 1], "gx", 1)
    ext_rows = extend(fields, above, row_count, 1)
    row_ok = jnp.arange(half_x, dtype=jnp.int32) >= half_x - row_count // 2
    col_count = cols_live[lax.axis_index("gy")]
    beside = from_behind(ext_rows[:, :, cap_y - 1], "gy", 1)
    ext_full = extend(ext_rows, beside, col_count, 2)
    lhs = ext_full[None]
    kernel = weight.reshape(out_chans, in_chans, 3, 3, 3)
    dims = ("NCDHW", "OIDHW", "NCDHW")
    conv = (
        lax.conv_general_dilated(
            lhs,
            kernel,
            (2, 2, 2),
            ((0, 0), (0, 0), (1, 0)),
            dimension_numbers=dims,
            preferred_element_type=jnp.float32,
        )[0]
        + bias[:, None, None, None]
    )
    col_ok = jnp.arange(half_y, dtype=jnp.int32) >= half_y - col_count // 2
    live = (row_ok[:, None] & col_ok[None, :]).reshape(1, half_x, half_y, 1)
    pre_local = jnp.where(live, conv, 0.0).astype(jnp.bfloat16)
    regrouped = lax.all_to_all(pre_local, "gy", split_axis=0, concat_axis=2, tiled=True)
    pre_wide = regrouped.astype(jnp.float32)
    sigma = jax.nn.sigmoid(pre_wide)
    stem = (pre_wide * sigma).astype(jnp.bfloat16)
    wide_cols = jnp.arange(half_y, dtype=jnp.int32)[None, :] >= half_y - (cols_live // 2)[:, None]
    wide_live = row_ok.reshape(1, half_x, 1, 1) & wide_cols.reshape(1, 1, tiles_y * half_y, 1)
    slope = sigma * (1.0 + pre_wide * (1.0 - sigma))
    grad_pre = jnp.where(wide_live, grad_out.astype(jnp.float32) * slope, 0.0).astype(jnp.bfloat16)
    returned = lax.all_to_all(grad_pre, "gy", split_axis=2, concat_axis=0, tiled=True)
    filt = lax.conv_general_dilated(
        ext_full[:, None],
        returned[:, None],
        (1, 1, 1),
        ((0, 0), (0, 0), (1, 0)),
        rhs_dilation=(2, 2, 2),
        dimension_numbers=dims,
        preferred_element_type=jnp.float32,
    )
    weight_full = jnp.swapaxes(filt, 0, 1).reshape(out_chans, -1)
    bias_full = jnp.sum(returned.astype(jnp.float32), axis=(1, 2, 3))
    packed = jnp.concatenate([weight_full, bias_full[:, None]], axis=1)
    total = lax.psum(packed, ("gx", "gy"))
    rows = out_chans // tiles_y
    mine = lax.dynamic_slice_in_dim(total, lax.axis_index("gy") * rows, rows, 0)
    weight_grad, bias_grad = (mine[:, :-1], mine[:, -1])
    return (stem, weight_grad, bias_grad)


def solution(mesh):
    in_specs = (P(None, "gx", "gy", None), P(), P(), P(), P(), P("gy", "gx", None, None))
    out_specs = (P("gy", "gx", None, None), P("gy", None), P("gy"))
    return jax.shard_map(local, mesh=mesh, in_specs=in_specs, out_specs=out_specs, check_vma=False)
```

profile of v0, /device:TPU:0, one launch (start us, length us, event | category | flops | bytes accessed | tf_op | source)
XLA Modules:
  0.0 264.5 jit_solution(15220797202595424917)
XLA Ops:
  0.6 0.9 slice_bitcast_fusion
  1.5 4.9 %collective-permute-start = (bf16[4,32,256]{2,1,0:T(8,128)(2,1)S(1)}, bf16[4,32,256]{2,1,0:T(8,128)(2,1)S(1)}, u32[]{:S(2)}, u32[]{:S(2)}) collective-permute-start(bf16[4,32,256]{2,1,0:T(8,128)(2,1)S(1)} %slice_bitcast_fusion), channel_id=1, source_target_pairs={{0,4},{4,8},{8,12},{12,16},{16,20},{20,24},{24,28},{1,5},{5,9},{9,... | collective-permute-start | bytes 196616 | tf_op jit(solution)/shard_map/ppermute | solution.py:10
  6.4 1.2 dynamic_slice.10
  10.2 1.2 dynamic_slice.9
  14.7 0.7 fusion.20
  16.1 0.1 broadcast_and_fusion.1
  16.1 0.0 collective-permute-done
  16.1 1.2 select_select_fusion.1
  17.4 1.5 collective-permute-start.1
  18.9 0.8 copy.105
  19.7 0.7 reshape.142
  20.4 0.0 collective-permute-done.1
  20.4 0.0 copy-start.6
  20.4 1.3 fusion.24
  21.7 0.5 pad.2
  22.2 2.2 reshape.158
  24.4 0.0 copy-start.3
  24.4 12.6 %copy.104 = bf16[4,9,33,1,8,34]{4,0,5,2,1,3:T(4,128)(2,1)} copy(bf16[4,9,33,1,8,34]{5,4,2,1,0,3:T(8,128)(2,1)S(1)} %reshape.158) | data formatting | bytes 1292544 | tf_op jit(solution)/shard_map/conv_general_dilated | solution.py:55
  37.0 1.5 slice.19
  38.5 0.0 copy-done.6
  38.5 0.0 copy-done.3
  38.5 14.1 %broadcast_select_fusion = f32[4,16,8,17,32]{4,2,3,1,0:T(8,128)S(1)} fusion(pred[8,17]{0,1:T(8,128)(4,1)S(1)} %copy-done.6, bf16[4,9,33,1,7,2]{4,0,5,2,1,3:T(4,128)(2,1)S(1)} %slice.19, bf16[4,9,33,1,8,34]{4,0,5,2,1,3:T(4,128)(2,1)} %copy.104, bf16[32,4,3,3,3]{0,4,3,2,1:T(4,128)(2,1)S(1)} %copy-done.3), kind=kOutput, calls=%fused_computation.6 | convolution fusion | flops 62493440 | bytes 1800696 | tf_op jit(solution)/shard_map/conv_general_dilated | solution.py:55
  52.6 0.0 copy-start.5
  52.6 0.8 copy.107
  53.4 0.0 copy-start.1
  53.4 0.0 copy-start
  53.4 2.2 slice.20
  55.6 3.5 %copy.121 = f32[4,16,1,128,32]{3,1,0,4,2:T(8,128)S(1)} copy(f32[4,16,1,128,32]{4,1,3,0,2:T(8,128)} %slice.20) | data formatting | bytes 2097152
  59.2 0.0 copy-done.5
  59.2 1.1 fusion.9
  60.2 4.9 %all-to-all-start = ((bf16[32,4,16,128]{3,2,1,0:T(8,128)(2,1)}), bf16[32,4,16,128]{3,2,1,0:T(8,128)(2,1)S(1)}, u32[]{:S(2)}, u32[]{:S(2)}) async-start(bf16[32,4,16,128]{3,2,1,0:T(8,128)(2,1)} %fusion.9), calls=%async_computation | async-start | bytes 1048576 | tf_op jit(solution)/shard_map/all_to_all | solution.py:68
  65.1 0.1 iota_compare_fusion.1
  65.2 0.1 ge.51
  65.3 0.1 broadcast_and_fusion
  65.4 8.6 %all-to-all-done = bf16[32,4,16,128]{3,2,1,0:T(8,128)(2,1)S(1)} async-done(((bf16[32,4,16,128]{3,2,1,0:T(8,128)(2,1)}), bf16[32,4,16,128]{3,2,1,0:T(8,128)(2,1)S(1)}, u32[]{:S(2)}, u32[]{:S(2)}) %all-to-all-start) | async-done | bytes 524320 | tf_op jit(solution)/shard_map/all_to_all | solution.py:68
  74.0 0.1 convert_bitcast_fusion
  74.1 0.1 copy.109
  74.2 0.0 copy-done.1
  74.2 1.3 fusion.18
  75.5 1.2 copy.110
  76.7 3.6 %all-to-all-start.1 = ((bf16[8,4,64,128]{3,1,0,2:T(4,128)(2,1)}), bf16[8,4,64,128]{3,1,0,2:T(4,128)(2,1)S(1)}, u32[]{:S(2)}, u32[]{:S(2)}) async-start(bf16[8,4,64,128]{3,1,0,2:T(4,128)(2,1)} %copy.110), calls=%async_computation.1 | async-start | bytes 1048576 | tf_op jit(solution)/shard_map/all_to_all | solution.py:76
  80.4 0.0 copy-done
  80.4 48.7 %copy.113 = bf16[4,1,9,33,256]{0,1,4,3,2:T(2,128)(2,1)} copy(bf16[4,1,9,33,256]{4,3,2,0,1:T(8,128)(2,1)S(1)} %copy-done) | data formatting | bytes 1216512 | tf_op jit(solution)/shard_map/broadcast_in_dim | solution.py:78
  129.1 0.0 all-to-all-done.1
  129.1 0.2 copy.111
  129.3 0.2 convert_reduce_fusion
  129.5 0.1 copy.112
  129.6 0.1 copy.116
  129.7 0.7 broadcast_in_dim.115
  130.4 4.8 %copy.114 = bf16[32,1,4,16,128]{0,1,4,3,2:T(2,128)(2,1)} copy(bf16[32,1,4,16,128]{4,3,2,0,1:T(8,128)(2,1)S(1)} %bitcast.72) | data formatting | bytes 1048576 | tf_op jit(solution)/shard_map/broadcast_in_dim | solution.py:79
  135.1 0.0 copy-start.2
  135.1 87.7 %fusion.26 = f32[32,4,3,3,3]{0,1,4,3,2:T(4,128)S(1)} fusion(bf16[4,1,9,33,256]{0,1,4,3,2:T(2,128)(2,1)} %copy.113, bf16[32,1,4,16,128]{0,1,4,3,2:T(2,128)(2,1)} %copy.114), kind=kOutput, calls=%fused_computation.51 | convolution fusion | flops 56475648 | bytes 1146368 | tf_op jit(solution)/shard_map/transpose | solution.py:86
  222.9 0.1 copy.117
  222.9 0.0 copy-done.2
  222.9 0.1 pad_maximum_fusion
  223.0 40.8 %psum.7 = f32[32,109]{1,0:T(8,128)S(1)} all-reduce(f32[32,109]{1,0:T(8,128)S(1)} %pad_maximum_fusion), channel_id=1, replica_groups=mesh['gx'=8,'gy'=4] {'gx','gy'}, use_global_device_ids=true, to_apply=%region_1.2 | all-reduce | flops 3488 | bytes 27904 | tf_op jit(solution)/shard_map/psum | solution.py:89
  263.8 0.0 copy-start.4
  263.8 0.7 slice_reduce_fusion
  264.5 0.0 copy-done.4
  (10 shorter events, 0.1 us)
Async XLA Ops:
  1.5 14.7 %collective-permute-start = (bf16[4,32,256]{2,1,0:T(8,128)(2,1)S(1)}, bf16[4,32,256]{2,1,0:T(8,128)(2,1)S(1)}, u32[]{:S(2)}, u32[]{:S(2)}) collective-permute-start(bf16[4,32,256]{2,1,0:T(8,128)(2,1)S(1)} %slice_bitcast_fusion), channel_id=1, source_target_pairs={{0,4},{4,8},{8,12},{12,16},{16,20},{20,24},{24,28},{1,5},{5,9},{9,... | collective-permute-start | bytes 196616 | tf_op jit(solution)/shard_map/ppermute | solution.py:10
  17.4 3.0 %collective-permute-start.1 = (bf16[4,9,256]{2,0,1:T(4,128)(2,1)S(1)}, bf16[4,9,256]{2,0,1:T(4,128)(2,1)S(1)}, u32[]{:S(2)}, u32[]{:S(2)}) collective-permute-start(bf16[4,9,256]{2,0,1:T(4,128)(2,1)S(1)} %bitcast.73), channel_id=1, source_target_pairs={{0,1},{1,2},{2,3},{4,5},{5,6},{6,7},{8,9},{9,10},{10,11},{12,13},{... | collective-permute-start | bytes 55304 | tf_op jit(solution)/shard_map/ppermute | solution.py:10
  20.4 18.1 %copy-start.6 = (pred[8,17]{0,1:T(8,128)(4,1)S(1)}, pred[8,17]{0,1:T(8,128)(4,1)}, u32[]{:S(2)}) copy-start(pred[8,17]{0,1:T(8,128)(4,1)} %constant.67) | copy-start | bytes 412
  24.4 14.1 %copy-start.3 = (bf16[32,4,3,3,3]{0,4,3,2,1:T(4,128)(2,1)S(1)}, bf16[32,4,3,3,3]{0,4,3,2,1:T(4,128)(2,1)}, u32[]{:S(2)}) copy-start(bf16[32,4,3,3,3]{0,4,3,2,1:T(4,128)(2,1)} %reshape.142) | copy-start | bytes 20740
  52.6 6.6 %copy-start.5 = (f32[32]{0:T(128)S(1)}, f32[32]{0:T(128)}, u32[]{:S(2)}) copy-start(f32[32]{0:T(128)} %param.10) | copy-start | bytes 388
  53.4 20.8 %copy-start.1 = (bf16[8,4,64,128]{3,2,1,0:T(8,128)(2,1)S(1)}, bf16[8,4,64,128]{3,2,1,0:T(8,128)(2,1)}, u32[]{:S(2)}) copy-start(bf16[8,4,64,128]{3,2,1,0:T(8,128)(2,1)} %param.11) | copy-start | bytes 1572868
  53.4 27.0 %copy-start = (bf16[4,1,9,33,256]{4,3,2,0,1:T(8,128)(2,1)S(1)}, bf16[4,1,9,33,256]{4,3,2,0,1:T(8,128)(2,1)}, u32[]{:S(2)}) copy-start(bf16[4,1,9,33,256]{4,3,2,0,1:T(8,128)(2,1)} %get-tuple-element.11) | copy-start | bytes 1824772
  60.2 13.7 %all-to-all-start = ((bf16[32,4,16,128]{3,2,1,0:T(8,128)(2,1)}), bf16[32,4,16,128]{3,2,1,0:T(8,128)(2,1)S(1)}, u32[]{:S(2)}, u32[]{:S(2)}) async-start(bf16[32,4,16,128]{3,2,1,0:T(8,128)(2,1)} %fusion.9), calls=%async_computation | async-start | bytes 1048576 | tf_op jit(solution)/shard_map/all_to_all | solution.py:68
  76.7 52.4 %all-to-all-start.1 = ((bf16[8,4,64,128]{3,1,0,2:T(4,128)(2,1)}), bf16[8,4,64,128]{3,1,0,2:T(4,128)(2,1)S(1)}, u32[]{:S(2)}, u32[]{:S(2)}) async-start(bf16[8,4,64,128]{3,1,0,2:T(4,128)(2,1)} %copy.110), calls=%async_computation.1 | async-start | bytes 1048576 | tf_op jit(solution)/shard_map/all_to_all | solution.py:76
  135.1 87.8 %copy-start.2 = (f32[32,1]{1,0:T(8,128)S(1)}, f32[32,1]{1,0:T(8,128)}, u32[]{:S(2)}) copy-start(f32[32,1]{1,0:T(8,128)} %broadcast_in_dim.115) | copy-start | bytes 388
  263.8 0.7 copy-start.4
where the time goes:
time: 265 us
  matrix products  102 us (38%)
  local copies, waits for them, and re-layouts  84.9 us (32%)
  blocking collectives  40.8 us (15%)
  starting transfers between devices  14.9 us (6%)
  waiting for transfers between devices  8.58 us (3%)
  between operations  7.43 us (3%)
  other arithmetic  6.22 us (2%)
    transpose x1, matrix products, local(): weight_full = jnp.swapaxes(filt, 0, 1).reshape(out_chans, -1)  87.7 us
    broadcast_in_dim x1, local copies, waits for them, and re-layouts, local(): ext_full[:, None]  48.7 us
    psum x1, blocking collectives, local(): total = lax.psum(packed, ('gx', 'gy'))  40.8 us
    conv_general_dilated x5, local copies, waits for them, and re-layouts, local(): lax.conv_general_dilated(lhs, kernel, (2, 2, 2), ((0, 0), (0, 0), (1, 0))...  19.2 us
    conv_general_dilated x1, matrix products, local(): lax.conv_general_dilated(lhs, kernel, (2, 2, 2), ((0, 0), (0, 0), (1, 0))...  14.1 us
    all_to_all x1, waiting for transfers between devices, local(): lax.all_to_all(pre_local, 'gy', split_axis=0, concat_axis=2, tiled=True)  8.57 us
    ppermute x2, starting transfers between devices, from_behind(): return lax.ppermute(block, axis, route)  6.32 us
  transfers between devices with their start and end apart: 4, of which 1 were waited for; matrix products, arithmetic and copies ran while one was open for 20% of the time, Pallas kernels for 0%

commit v1 on v0

--- a/solution.py
+++ b/solution.py
@@ -65,7 +65,10 @@
     col_ok = jnp.arange(half_y, dtype=jnp.int32) >= half_y - col_count // 2
     live = (row_ok[:, None] & col_ok[None, :]).reshape(1, half_x, half_y, 1)
     pre_local = jnp.where(live, conv, 0.0).astype(jnp.bfloat16)
-    regrouped = lax.all_to_all(pre_local, "gy", split_axis=0, concat_axis=2, tiled=True)
+    regrouped = jnp.concatenate(
+        lax.all_to_all(jnp.stack(jnp.split(pre_local, lax.axis_size("gy"), axis=0)), "gy", 0, 0),
+        axis=2,
+    )
     pre_wide = regrouped.astype(jnp.float32)
     sigma = jax.nn.sigmoid(pre_wide)
     stem = (pre_wide * sigma).astype(jnp.bfloat16)

time: 265 us -> 276 us (1.042)
  local copies, waits for them, and re-layouts: 84.9 us -> 94.4 us
    another operation x0 -> x5, local copies, waits for them, and re-layouts: none -> 16.2 us  [local(): jnp.stack(jnp.split(pre_local, lax.axis_size('gy'), axis=0))]
    unnamed x16 -> x15, local copies, waits for them, and re-layouts: 4.38 us -> 0.85 us
    conv_general_dilated x5 -> x4, local copies, waits for them, and re-layouts: 19.2 us -> 17.1 us  [local(): lax.conv_general_dilated(lhs, kernel, (2, 2, 2), ((0, 0), (0, 0), (1, 0))...]
  transfers between devices with their start and end apart: 4 -> 4, of which waited for: 1 -> 1; matrix products, arithmetic and copies ran while one was open for 20% -> 19% of each run, Pallas kernels for 0% -> 0%
where the time goes in v1:
time: 276 us; the launch traced here: 275 us
  matrix products  102 us (37%)
  local copies, waits for them, and re-layouts  94.4 us (34%)
  blocking collectives  41 us (15%)
  starting transfers between devices  14.7 us (5%)
  waiting for transfers between devices  8.58 us (3%)
  other arithmetic  7.43 us (3%)
  between operations  7.4 us (3%)
    transpose x1, matrix products, local(): weight_full = jnp.swapaxes(filt, 0, 1).reshape(out_chans, -1)  87.7 us
    broadcast_in_dim x1, local copies, waits for them, and re-layouts, local(): ext_full[:, None]  48 us
    psum x1, blocking collectives, local(): total = lax.psum(packed, ('gx', 'gy'))  41 us
    conv_general_dilated x4, local copies, waits for them, and re-layouts, local(): lax.conv_general_dilated(lhs, kernel, (2, 2, 2), ((0, 0), (0, 0), (1, 0))...  17.1 us
    another operation x5, local copies, waits for them, and re-layouts, local(): jnp.stack(jnp.split(pre_local, lax.axis_size('gy'), axis=0))  16.2 us
    conv_general_dilated x1, matrix products, local(): lax.conv_general_dilated(lhs, kernel, (2, 2, 2), ((0, 0), (0, 0), (1, 0))...  14.1 us
    all_to_all x1, waiting for transfers between devices, local(): lax.all_to_all(jnp.stack(jnp.split(pre_local, lax.axis_size('gy'), axis=0...  8.57 us
    ppermute x2, starting transfers between devices, from_behind(): return lax.ppermute(block, axis, route)  6.32 us
  transfers between devices with their start and end apart: 4, of which 1 were waited for; matrix products, arithmetic and copies ran while one was open for 19% of the time, Pallas kernels for 0%

profile of v1, /device:TPU:0, one launch (start us, length us, event | category | flops | bytes accessed | tf_op | source)
XLA Modules:
  0.0 275.3 jit_solution(12574723619589855716)
XLA Ops:
  0.6 0.9 slice_bitcast_fusion.5
  1.5 4.9 %collective-permute-start = (bf16[4,32,256]{2,1,0:T(8,128)(2,1)S(1)}, bf16[4,32,256]{2,1,0:T(8,128)(2,1)S(1)}, u32[]{:S(2)}, u32[]{:S(2)}) collective-permute-start(bf16[4,32,256]{2,1,0:T(8,128)(2,1)S(1)} %slice_bitcast_fusion.5), channel_id=1, source_target_pairs={{0,4},{4,8},{8,12},{12,16},{16,20},{20,24},{24,28},{1,5},{5,9},{9,... | collective-permute-start | bytes 196616 | tf_op jit(solution)/shard_map/ppermute | solution.py:10
  6.4 1.2 dynamic_slice.9
  10.8 0.7 fusion.21
  11.5 1.2 dynamic_slice.10
  16.1 0.1 broadcast_and_fusion.1
  16.1 0.0 collective-permute-done
  16.1 1.2 select_select_fusion.1
  17.4 1.5 collective-permute-start.1
  18.9 0.8 copy.93
  19.7 0.7 reshape.142
  20.3 0.0 collective-permute-done.1
  20.4 1.3 fusion.25
  21.7 0.5 pad.2
  22.2 2.2 reshape.157
  24.3 0.0 copy-start.3
  24.4 0.0 copy-start.6
  24.4 12.6 %copy.92 = bf16[4,9,33,1,8,34]{4,0,5,2,1,3:T(4,128)(2,1)} copy(bf16[4,9,33,1,8,34]{5,4,2,1,0,3:T(8,128)(2,1)S(1)} %reshape.157) | data formatting | bytes 1292544 | tf_op jit(solution)/shard_map/conv_general_dilated | solution.py:55
  37.0 1.5 slice.19
  38.5 0.0 copy-done.3
  38.5 0.0 copy-done.6
  38.5 14.1 %broadcast_select_fusion = f32[4,16,8,17,32]{4,2,3,1,0:T(8,128)S(1)} fusion(pred[8,17]{0,1:T(8,128)(4,1)S(1)} %copy-done.6, bf16[4,9,33,1,7,2]{4,0,5,2,1,3:T(4,128)(2,1)S(1)} %slice.19, bf16[4,9,33,1,8,34]{4,0,5,2,1,3:T(4,128)(2,1)} %copy.92, bf16[32,4,3,3,3]{0,4,3,2,1:T(4,128)(2,1)S(1)} %copy-done.3), kind=kOutput, calls=%fused_computation.10 | convolution fusion | flops 62493440 | bytes 1800696 | tf_op jit(solution)/shard_map/conv_general_dilated | solution.py:55
  52.6 0.0 copy-start.5
  52.6 0.8 copy.95
  53.4 0.0 copy-done.5
  53.4 0.5 fusion.8
  53.9 3.6 %slice_bitcast_fusion.4 = (bf16[1,8,4,16,128]{1,3,4,2,0:T(8,128)(2,1)S(1)}, bf16[1,8,4,16,128]{1,3,4,2,0:T(8,128)(2,1)}, bf16[1,8,4,16,128]{1,3,4,2,0:T(8,128)(2,1)}, bf16[1,8,4,16,128]{1,3,4,2,0:T(8,128)(2,1)}) fusion(bf16[32,4,16,128]{0,2,3,1:T(8,128)(2,1)S(1)} %fusion.8), kind=kLoop, calls=%fused_computation.14 | loop fusion | bytes 1048576 | tf_op jit(solution)/shard_map/stack | solution.py:69
  57.6 3.0 %copy.99 = bf16[1,8,4,16,128]{4,3,2,1,0:T(8,128)(2,1)S(1)} copy(bf16[1,8,4,16,128]{1,3,4,2,0:T(8,128)(2,1)} %get-tuple-element.10) | data formatting | bytes 262144 | tf_op jit(solution)/shard_map/stack | solution.py:69
  60.5 0.0 copy-start.1
  60.5 3.6 %copy.98 = bf16[1,8,4,16,128]{4,3,2,1,0:T(8,128)(2,1)} copy(bf16[1,8,4,16,128]{1,3,4,2,0:T(8,128)(2,1)} %get-tuple-element.11) | data formatting | bytes 262144 | tf_op jit(solution)/shard_map/stack | solution.py:69
  64.2 3.6 %copy.97 = bf16[1,8,4,16,128]{4,3,2,1,0:T(8,128)(2,1)} copy(bf16[1,8,4,16,128]{1,3,4,2,0:T(8,128)(2,1)} %get-tuple-element.12) | data formatting | bytes 262144 | tf_op jit(solution)/shard_map/stack | solution.py:69
  67.7 0.0 copy-start
  67.7 2.4 copy.96
  70.1 1.9 pad_maximum_fusion
  72.0 4.9 %all-to-all-start = ((bf16[4,8,4,16,128]{4,3,2,1,0:T(8,128)(2,1)}), bf16[4,8,4,16,128]{4,3,2,1,0:T(8,128)(2,1)S(1)}, u32[]{:S(2)}, u32[]{:S(2)}) async-start(bf16[4,8,4,16,128]{4,3,2,1,0:T(8,128)(2,1)} %pad_maximum_fusion), calls=%async_computation | async-start | bytes 1048576 | tf_op jit(solution)/shard_map/all_to_all | solution.py:69
  76.9 0.1 iota_compare_fusion.1
  77.0 0.1 ge.51
  77.1 0.1 broadcast_and_fusion
  77.1 8.6 %all-to-all-done = bf16[4,8,4,16,128]{4,3,2,1,0:T(8,128)(2,1)S(1)} async-done(((bf16[4,8,4,16,128]{4,3,2,1,0:T(8,128)(2,1)}), bf16[4,8,4,16,128]{4,3,2,1,0:T(8,128)(2,1)S(1)}, u32[]{:S(2)}, u32[]{:S(2)}) %all-to-all-start) | async-done | bytes 524320 | tf_op jit(solution)/shard_map/all_to_all | solution.py:69
  85.7 0.0 copy-done.1
  85.7 1.3 fusion.19
  87.1 1.2 copy.101
  88.3 3.5 %all-to-all-start.1 = ((bf16[8,4,64,128]{3,1,0,2:T(4,128)(2,1)}), bf16[8,4,64,128]{3,1,0,2:T(4,128)(2,1)S(1)}, u32[]{:S(2)}, u32[]{:S(2)}) async-start(bf16[8,4,64,128]{3,1,0,2:T(4,128)(2,1)} %copy.101), calls=%async_computation.1 | async-start | bytes 1048576 | tf_op jit(solution)/shard_map/all_to_all | solution.py:79
  91.7 0.0 copy-done
  91.8 48.0 %copy.104 = bf16[4,1,9,33,256]{0,1,4,3,2:T(2,128)(2,1)} copy(bf16[4,1,9,33,256]{4,3,2,0,1:T(8,128)(2,1)S(1)} %copy-done) | data formatting | bytes 1216512 | tf_op jit(solution)/shard_map/broadcast_in_dim | solution.py:81
  139.7 0.0 all-to-all-done.1
  139.7 0.2 copy.102
  140.0 0.2 convert_reduce_fusion
  140.2 0.1 copy.103
  140.2 0.1 copy.107
  140.3 0.7 broadcast_in_dim.115
  141.0 4.7 %copy.105 = bf16[32,1,4,16,128]{0,1,4,3,2:T(2,128)(2,1)} copy(bf16[32,1,4,16,128]{4,3,2,0,1:T(8,128)(2,1)S(1)} %bitcast.79) | data formatting | bytes 1048576 | tf_op jit(solution)/shard_map/broadcast_in_dim | solution.py:82
  145.7 0.0 copy-start.2
  145.7 87.7 %fusion.27 = f32[32,4,3,3,3]{0,1,4,3,2:T(4,128)S(1)} fusion(bf16[4,1,9,33,256]{0,1,4,3,2:T(2,128)(2,1)} %copy.104, bf16[32,1,4,16,128]{0,1,4,3,2:T(2,128)(2,1)} %copy.105), kind=kOutput, calls=%fused_computation.56 | convolution fusion | flops 56475648 | bytes 1146368 | tf_op jit(solution)/shard_map/transpose | solution.py:89
  233.5 0.1 copy.108
  233.5 0.0 copy-done.2
  233.5 0.1 pad_maximum_fusion.1
  233.6 41.0 %psum.7 = f32[32,109]{1,0:T(8,128)S(1)} all-reduce(f32[32,109]{1,0:T(8,128)S(1)} %pad_maximum_fusion.1), channel_id=1, replica_groups=mesh['gx'=8,'gy'=4] {'gx','gy'}, use_global_device_ids=true, to_apply=%region_1.2 | all-reduce | flops 3488 | bytes 27904 | tf_op jit(solution)/shard_map/psum | solution.py:92
  274.6 0.0 copy-start.4
  274.6 0.7 slice_reduce_fusion
  275.3 0.0 copy-done.4
  (10 shorter events, 0.1 us)
Async XLA Ops:
  1.5 14.7 %collective-permute-start = (bf16[4,32,256]{2,1,0:T(8,128)(2,1)S(1)}, bf16[4,32,256]{2,1,0:T(8,128)(2,1)S(1)}, u32[]{:S(2)}, u32[]{:S(2)}) collective-permute-start(bf16[4,32,256]{2,1,0:T(8,128)(2,1)S(1)} %slice_bitcast_fusion.5), channel_id=1, source_target_pairs={{0,4},{4,8},{8,12},{12,16},{16,20},{20,24},{24,28},{1,5},{5,9},{9,... | collective-permute-start | bytes 196616 | tf_op jit(solution)/shard_map/ppermute | solution.py:10
  17.4 3.0 %collective-permute-start.1 = (bf16[4,9,256]{2,0,1:T(4,128)(2,1)S(1)}, bf16[4,9,256]{2,0,1:T(4,128)(2,1)S(1)}, u32[]{:S(2)}, u32[]{:S(2)}) collective-permute-start(bf16[4,9,256]{2,0,1:T(4,128)(2,1)S(1)} %bitcast.80), channel_id=1, source_target_pairs={{0,1},{1,2},{2,3},{4,5},{5,6},{6,7},{8,9},{9,10},{10,11},{12,13},{... | collective-permute-start | bytes 55304 | tf_op jit(solution)/shard_map/ppermute | solution.py:10
  24.3 14.1 %copy-start.3 = (bf16[32,4,3,3,3]{0,4,3,2,1:T(4,128)(2,1)S(1)}, bf16[32,4,3,3,3]{0,4,3,2,1:T(4,128)(2,1)}, u32[]{:S(2)}) copy-start(bf16[32,4,3,3,3]{0,4,3,2,1:T(4,128)(2,1)} %reshape.142) | copy-start | bytes 20740
  24.4 14.1 %copy-start.6 = (pred[8,17]{0,1:T(8,128)(4,1)S(1)}, pred[8,17]{0,1:T(8,128)(4,1)}, u32[]{:S(2)}) copy-start(pred[8,17]{0,1:T(8,128)(4,1)} %constant.67) | copy-start | bytes 412
  52.6 0.8 copy-start.5
  60.5 25.2 %copy-start.1 = (bf16[8,4,64,128]{3,2,1,0:T(8,128)(2,1)S(1)}, bf16[8,4,64,128]{3,2,1,0:T(8,128)(2,1)}, u32[]{:S(2)}) copy-start(bf16[8,4,64,128]{3,2,1,0:T(8,128)(2,1)} %param.11) | copy-start | bytes 1572868
  67.7 24.0 %copy-start = (bf16[4,1,9,33,256]{4,3,2,0,1:T(8,128)(2,1)S(1)}, bf16[4,1,9,33,256]{4,3,2,0,1:T(8,128)(2,1)}, u32[]{:S(2)}) copy-start(bf16[4,1,9,33,256]{4,3,2,0,1:T(8,128)(2,1)} %get-tuple-element.13) | copy-start | bytes 1824772
  72.0 13.7 %all-to-all-start = ((bf16[4,8,4,16,128]{4,3,2,1,0:T(8,128)(2,1)}), bf16[4,8,4,16,128]{4,3,2,1,0:T(8,128)(2,1)S(1)}, u32[]{:S(2)}, u32[]{:S(2)}) async-start(bf16[4,8,4,16,128]{4,3,2,1,0:T(8,128)(2,1)} %pad_maximum_fusion), calls=%async_computation | async-start | bytes 1048576 | tf_op jit(solution)/shard_map/all_to_all | solution.py:69
  88.3 51.5 %all-to-all-start.1 = ((bf16[8,4,64,128]{3,1,0,2:T(4,128)(2,1)}), bf16[8,4,64,128]{3,1,0,2:T(4,128)(2,1)S(1)}, u32[]{:S(2)}, u32[]{:S(2)}) async-start(bf16[8,4,64,128]{3,1,0,2:T(4,128)(2,1)} %copy.101), calls=%async_computation.1 | async-start | bytes 1048576 | tf_op jit(solution)/shard_map/all_to_all | solution.py:79
  145.7 87.8 %copy-start.2 = (f32[32,1]{1,0:T(8,128)S(1)}, f32[32,1]{1,0:T(8,128)}, u32[]{:S(2)}) copy-start(f32[32,1]{1,0:T(8,128)} %broadcast_in_dim.115) | copy-start | bytes 388
  274.6 0.7 copy-start.4
